TPU v7x, 512 devices: a whole 4x4x16 slice. The times are simulated.
512 devices in a mesh: filt: 64 (over y, x, z_hi), slab: 8 (over z_lo, core).
Axes of the slice: x: 4, y: 4, z: 16 (z_hi: 4, z_lo: 4; z = z_hi * 4 + z_lo), core: 2. Of those that a mesh axis runs over, the one named last changes fastest.
Arguments:
- activations: bfloat16 [2048, 16, 512], P('filt', 'slab'), may hold values from -6 to 6
- grad_out: bfloat16 [2048, 16, 512], P('filt', 'slab'), may hold values from -6 to 6
- weights: bfloat16 [27, 256, 256], P(None, 'filt'), may hold values from -0.078125 to 0.078125
Outputs:
- out_map: bfloat16 [2048, 16, 512], P('filt', 'slab')
- grad_in: bfloat16 [2048, 16, 512], P('filt', 'slab')
- filter_grad: float32 [27, 256, 256], P(None, 'filt')
All inputs are finite; a program needn't handle non-finite values.
Results may differ from a plain program's by a relative error of at most 0.001.
Values may be sent and summed in bfloat16 or wider, within the bound.
No kernel may reach another device: no remote copies, remote signals or barrier semaphores. Data moves between devices by JAX's collectives and lax.ppermute only.
A program may use at most 64 MiB of HBM per device.

v0:
```python
import math
import jax
import jax.numpy as jnp
from jax import lax
from jax.sharding import Mesh
from jax.sharding import PartitionSpec as P

CH_IN = 256
CH_OUT = 256
GROUPS = 8
ROWS = 8
WIDTH = 64


def from_offset(value, d_rb, d_slab, n_rb, n_slab):
    if d_slab == 0:
        pairs = [(r + d_rb, r) for r in range(n_rb) if 0 <= r + d_rb < n_rb]
        return lax.ppermute(value, "rb", pairs)
    if d_rb == 0:
        pairs = [(s + d_slab, s) for s in range(n_slab) if 0 <= s + d_slab < n_slab]
        return lax.ppermute(value, "slab", pairs)
    pairs = []
    for r in range(n_rb):
        for s in range(n_slab):
            if 0 <= r + d_rb < n_rb and 0 <= s + d_slab < n_slab:
                pairs.append(((r + d_rb) * n_slab + s + d_slab, r * n_slab + s))
    return lax.ppermute(value, ("rb", "slab"), pairs)


def haloed(block):
    n_rb = lax.axis_size("rb")
    n_slab = lax.axis_size("slab")

    def part(d_rb, d_slab):
        piece = block
        if d_slab < 0:
            piece = piece[:, -1:]
        elif d_slab > 0:
            piece = piece[:, :1]
        if d_rb < 0:
            piece = piece[:, :, -1:]
        elif d_rb > 0:
            piece = piece[:, :, :1]
        if d_rb == 0 and d_slab == 0:
            return piece
        return from_offset(piece, d_rb, d_slab, n_rb, n_slab)

    planes = []
    for d_slab in (-1, 0, 1):
        planes.append(jnp.concatenate([part(d_rb, d_slab) for d_rb in (-1, 0, 1)], axis=2))
    return jnp.concatenate(planes, axis=1)


def correlate(image, kernel, lhs_spec):
    return lax.conv_general_dilated(
        image,
        kernel,
        (1, 1, 1),
        ((0, 0), (0, 0), (1, 1)),
        dimension_numbers=(lhs_spec, "OIDHW", "NCDHW"),
        preferred_element_type=jnp.float32,
    )


def per_device(activations, grad_out, weights):
    chan_local = activations.shape[0]
    depth_dev = activations.shape[1]
    n_rb = lax.axis_size("rb")
    depth_all = depth_dev * lax.axis_size("slab")
    height_all = ROWS * n_rb
    both = jnp.concatenate([activations, grad_out], axis=0).reshape(
        2 * chan_local, depth_dev, ROWS, WIDTH
    )
    whole = lax.all_gather(haloed(both), "grp", axis=0, tiled=False)
    whole_in = whole[:, :chan_local].reshape((CH_IN,) + whole.shape[2:])
    whole_grad = whole[:, chan_local:].reshape((CH_OUT,) + whole.shape[2:])
    group_weights = lax.all_gather(weights, "rb", axis=1, tiled=True)
    column_weights = lax.all_to_all(group_weights, "grp", split_axis=2, concat_axis=1, tiled=True)
    out_kernel = jnp.transpose(group_weights, (1, 2, 0)).reshape(chan_local, CH_IN, 3, 3, 3)
    output_sum = correlate(whole_in[None], out_kernel, "NCDHW")
    grad_kernel = grad_out.reshape(chan_local, 1, depth_dev, ROWS, WIDTH)
    filter_terms = correlate(whole_in[:, None], grad_kernel, "NCDHW")
    filter_part = jnp.transpose(filter_terms.reshape(CH_IN, chan_local, 27), (2, 1, 0))
    in_kernel = jnp.transpose(column_weights[::-1], (2, 1, 0)).reshape(chan_local, CH_OUT, 3, 3, 3)
    input_sum = correlate(whole_grad[None], in_kernel, "NCDHW")
    scale_factor = 1.0 / math.sqrt(depth_all * height_all * WIDTH)
    rows_part = lax.psum_scatter(filter_part, "rb", scatter_dimension=1, tiled=True)
    filter_grad = lax.psum(rows_part, "slab") * scale_factor
    out_map = output_sum.astype(jnp.bfloat16).reshape(chan_local, depth_dev, ROWS * WIDTH)
    grad_in = input_sum.astype(jnp.bfloat16).reshape(chan_local, depth_dev, ROWS * WIDTH)
    return (out_map, grad_in, filter_grad)


def solution(mesh):
    n_filt, n_slab = mesh.devices.shape
    grid = Mesh(mesh.devices.reshape(n_filt // GROUPS, GROUPS, n_slab), ("rb", "grp", "slab"))
    act_spec = P(("rb", "grp"), "slab", None)
    w_spec = P(None, ("rb", "grp"), None)
    in_specs = (act_spec, act_spec, w_spec)
    out_specs = (act_spec, act_spec, w_spec)
    return jax.shard_map(
        per_device, mesh=grid, in_specs=in_specs, out_specs=out_specs, check_vma=False
    )
```

profile of v0, /device:TPU:1, one launch (start us, length us, event | category | flops | bytes accessed | tf_op | source)
XLA Modules:
  0.0 521.8 jit_solution(6389303513420632866)
XLA Ops:
  8.6 7.4 %collective-permute-start = (bf16[64,1,1,64]{3,2,0,1:T(2,128)(2,1)S(1)}, bf16[64,1,1,64]{3,2,0,1:T(2,128)(2,1)S(1)}, u32[]{:S(2)}, u32[]{:S(2)}) collective-permute-start(bf16[64,1,1,64]{3,2,0,1:T(2,128)(2,1)S(1)} %get-tuple-element.14), channel_id=1, source_target_pairs={{0,65},{1,66},{2,67},{3,68},{4,69},{5,70},{6,71},{64,129},{65,130}... | collective-permute-start | bytes 24584 | tf_op jit(solution)/shard_map/ppermute | solution.py:27
  16.0 1.3 collective-permute-start.2
  17.3 5.8 %collective-permute-start.5 = (bf16[64,1,1,64]{3,2,0,1:T(2,128)(2,1)S(1)}, bf16[64,1,1,64]{3,2,0,1:T(2,128)(2,1)S(1)}, u32[]{:S(2)}, u32[]{:S(2)}) collective-permute-start(bf16[64,1,1,64]{3,2,0,1:T(2,128)(2,1)S(1)} %get-tuple-element.16), channel_id=1, source_target_pairs={{1,64},{2,65},{3,66},{4,67},{5,68},{6,69},{7,70},{65,128},{66,129}... | collective-permute-start | bytes 24584 | tf_op jit(solution)/shard_map/ppermute | solution.py:27
  23.1 2.8 collective-permute-start.1
  25.9 1.9 collective-permute-start.6
  27.9 4.1 collective-permute-start.3
  32.0 1.3 collective-permute-start.4
  33.3 1.4 collective-permute-start.7
  34.7 7.8 %collective-permute-done.7 = bf16[64,1,1,64]{3,2,0,1:T(2,128)(2,1)S(1)} collective-permute-done((bf16[64,1,1,64]{3,2,0,1:T(2,128)(2,1)S(1)}, bf16[64,1,1,64]{3,2,0,1:T(2,128)(2,1)S(1)}, u32[]{:S(2)}, u32[]{:S(2)}) %collective-permute-start.7) | collective-permute-done | bytes 8224 | tf_op jit(solution)/shard_map/ppermute | solution.py:27
  43.2 1.7 copy.57
  45.0 31.7 %all_gather.11 = bf16[27,32,256]{2,0,1:T(8,128)(2,1)S(1)} all-gather(bf16[27,4,256]{2,0,1:T(8,128)(2,1)S(1)} %copy.62), channel_id=1, replica_groups=mesh['rb'=8,'grp'=8,'slab'=8] {'rb'}, dimensions={1}, use_global_device_ids=true | all-gather | bytes 497664 | tf_op jit(solution)/shard_map/all_gather | solution.py:77
  76.7 3.2 copy.70
  80.0 2.1 reshape.64
  82.1 14.7 %all-to-all-start = ((bf16[8,2,13824]{2,1,0:T(2,128)(2,1)}), bf16[8,2,13824]{2,1,0:T(2,128)(2,1)S(1)}, u32[]{:S(2)}, u32[]{:S(2)}) async-start(bf16[8,2,13824]{2,1,0:T(2,128)(2,1)} %reshape.64), calls=%async_computation | async-start | bytes 884736 | tf_op jit(solution)/shard_map/all_to_all | solution.py:78
  100.7 99.3 %all-to-all-done = bf16[8,2,13824]{2,1,0:T(2,128)(2,1)S(1)} async-done(((bf16[8,2,13824]{2,1,0:T(2,128)(2,1)}), bf16[8,2,13824]{2,1,0:T(2,128)(2,1)S(1)}, u32[]{:S(2)}, u32[]{:S(2)}) %all-to-all-start) | async-done | bytes 442400 | tf_op jit(solution)/shard_map/all_to_all | solution.py:78
  200.0 1.6 reshape.65
  201.6 2.4 copy.89
  204.0 2.8 all_to_all.16
  207.6 81.8 %all-gather.3.cloned.1.call-done = bf16[512,4,10,64]{3,1,2,0:T(4,128)(2,1)} async-done(((bf16[64,4,10,64]{3,1,2,0:T(4,128)(2,1)}), bf16[512,4,10,64]{3,1,2,0:T(4,128)(2,1)}) %all-gather.3.cloned.1.call-update) | async-done | bytes 2621456 | tf_op jit(solution)/shard_map/all_gather | solution.py:74
  289.4 5.9 %fusion.36 = (bf16[8,32,4,10,64]{4,2,3,1,0:T(4,128)(2,1)}, bf16[8,32,4,10,64]{4,2,3,1,0:T(4,128)(2,1)S(1)}) fusion(bf16[8,64,4,10,64]{4,2,3,1,0:T(4,128)(2,1)} %bitcast.65), kind=kLoop, calls=%fused_computation.34 | loop fusion | bytes 5242880 | tf_op jit(solution)/shard_map/slice | solution.py:76
  296.0 2.5 copy.86
  298.4 1.9 pad.clone
  301.8 5.5 %copy.74 = bf16[256,1,4,10,64]{0,1,4,3,2:T(2,128)(2,1)} copy(bf16[256,1,4,10,64]{4,0,3,2,1:T(8,128)(2,1)S(1)} %bitcast.58) | data formatting | bytes 2621440 | tf_op jit(solution)/shard_map/broadcast_in_dim;reshape | solution.py:82
  307.3 18.5 %fusion.40 = f32[256,32,3,3,3]{0,1,4,3,2:T(8,128)} fusion(bf16[256,1,4,10,64]{0,1,4,3,2:T(2,128)(2,1)} %copy.74, bf16[32,1,2,8,64]{0,1,4,3,2:T(2,128)(2,1)S(1)} %copy.75), kind=kOutput, calls=%fused_computation.38 | convolution fusion | flops 448266240 | bytes 2260992 | tf_op jit(solution)/shard_map/conv_general_dilated | solution.py:55
  325.9 4.3 fusion.22
  330.8 2.7 copy.87
  333.5 1.9 pad.2.clone
  336.5 4.3 fusion.25
  340.8 87.6 %all-reduce.6.cloned.1.call-done = f32[27,32,256]{2,1,0:T(8,128)} async-done(((f32[27,32,256]{2,1,0:T(8,128)}), f32[27,32,256]{2,1,0:T(8,128)}) %all-reduce.6.cloned.1.call-update) | async-done | bytes 884752
  428.4 1.6 constant_dynamic-slice_fusion
  432.1 81.4 %all-reduce.4.cloned.1.call-done = f32[27,4,256]{2,1,0:T(4,128)} async-done(((f32[27,4,256]{2,1,0:T(4,128)}), f32[27,4,256]{2,1,0:T(4,128)}) %all-reduce.4.cloned.1.call-update) | async-done | bytes 110608 | tf_op jit(solution)/shard_map/psum | solution.py:88
  513.5 1.6 broadcast_multiply_fusion
  (56 shorter events, 12.1 us)
Async XLA Ops:
  7.2 282.2 %all-gather.3.cloned.1.call-start = ((), (), s32[]{:S(2)}) async-start(), calls=%async_computation.2 | async-start | bytes 5898240 | tf_op jit(solution)/shard_map/all_gather | solution.py:74
  8.6 19.3 %collective-permute-start = (bf16[64,1,1,64]{3,2,0,1:T(2,128)(2,1)S(1)}, bf16[64,1,1,64]{3,2,0,1:T(2,128)(2,1)S(1)}, u32[]{:S(2)}, u32[]{:S(2)}) collective-permute-start(bf16[64,1,1,64]{3,2,0,1:T(2,128)(2,1)S(1)} %get-tuple-element.14), channel_id=1, source_target_pairs={{0,65},{1,66},{2,67},{3,68},{4,69},{5,70},{6,71},{64,129},{65,130}... | collective-permute-start | bytes 24584 | tf_op jit(solution)/shard_map/ppermute | solution.py:27
  16.0 16.0 %collective-permute-start.2 = (bf16[64,1,1,64]{3,2,0,1:T(2,128)(2,1)S(1)}, bf16[64,1,1,64]{3,2,0,1:T(2,128)(2,1)S(1)}, u32[]{:S(2)}, u32[]{:S(2)}) collective-permute-start(bf16[64,1,1,64]{3,2,0,1:T(2,128)(2,1)S(1)} %get-tuple-element.17), channel_id=1, source_target_pairs={{64,1},{65,2},{66,3},{67,4},{68,5},{69,6},{70,7},{128,65},{129,66}... | collective-permute-start | bytes 24584 | tf_op jit(solution)/shard_map/ppermute | solution.py:27
  17.3 16.0 %collective-permute-start.5 = (bf16[64,1,1,64]{3,2,0,1:T(2,128)(2,1)S(1)}, bf16[64,1,1,64]{3,2,0,1:T(2,128)(2,1)S(1)}, u32[]{:S(2)}, u32[]{:S(2)}) collective-permute-start(bf16[64,1,1,64]{3,2,0,1:T(2,128)(2,1)S(1)} %get-tuple-element.16), channel_id=1, source_target_pairs={{1,64},{2,65},{3,66},{4,67},{5,68},{6,69},{7,70},{65,128},{66,129}... | collective-permute-start | bytes 24584 | tf_op jit(solution)/shard_map/ppermute | solution.py:27
  23.1 19.5 %collective-permute-start.1 = (bf16[64,1,8,64]{3,2,0,1:T(8,128)(2,1)S(1)}, bf16[64,1,8,64]{3,2,0,1:T(8,128)(2,1)S(1)}, u32[]{:S(2)}, u32[]{:S(2)}) collective-permute-start(bf16[64,1,8,64]{3,2,0,1:T(8,128)(2,1)S(1)} %get-tuple-element.18), channel_id=1, source_target_pairs={{0,1},{1,2},{2,3},{3,4},{4,5},{5,6},{6,7},{8,9},{9,10},{10,11},{11... | collective-permute-start | bytes 196616 | tf_op jit(solution)/shard_map/ppermute | solution.py:21
  25.9 16.7 %collective-permute-start.6 = (bf16[64,1,8,64]{3,2,0,1:T(8,128)(2,1)S(1)}, bf16[64,1,8,64]{3,2,0,1:T(8,128)(2,1)S(1)}, u32[]{:S(2)}, u32[]{:S(2)}) collective-permute-start(bf16[64,1,8,64]{3,2,0,1:T(8,128)(2,1)S(1)} %get-tuple-element.19), channel_id=1, source_target_pairs={{1,0},{2,1},{3,2},{4,3},{5,4},{6,5},{7,6},{9,8},{10,9},{11,10},{12... | collective-permute-start | bytes 196616 | tf_op jit(solution)/shard_map/ppermute | solution.py:21
  27.9 14.6 %collective-permute-start.3 = (bf16[64,2,1,64]{3,2,0,1:T(2,128)(2,1)S(1)}, bf16[64,2,1,64]{3,2,0,1:T(2,128)(2,1)S(1)}, u32[]{:S(2)}, u32[]{:S(2)}) collective-permute-start(bf16[64,2,1,64]{3,2,0,1:T(2,128)(2,1)S(1)} %get-tuple-element.20), channel_id=1, source_target_pairs={{0,64},{64,128},{128,192},{192,256},{256,320},{320,384},{384,448},... | collective-permute-start | bytes 49160 | tf_op jit(solution)/shard_map/ppermute | solution.py:18
  32.0 10.6 %collective-permute-start.4 = (bf16[64,2,1,64]{3,2,0,1:T(2,128)(2,1)S(1)}, bf16[64,2,1,64]{3,2,0,1:T(2,128)(2,1)S(1)}, u32[]{:S(2)}, u32[]{:S(2)}) collective-permute-start(bf16[64,2,1,64]{3,2,0,1:T(2,128)(2,1)S(1)} %get-tuple-element.21), channel_id=1, source_target_pairs={{64,0},{128,64},{192,128},{256,192},{320,256},{384,320},{448,384},... | collective-permute-start | bytes 49160 | tf_op jit(solution)/shard_map/ppermute | solution.py:18
  33.3 11.6 %copy-start.6 = (bf16[27,4,256]{2,1,0:T(4,128)(2,1)S(1)}, bf16[27,4,256]{2,1,0:T(4,128)(2,1)}, u32[]{:S(2)}) copy-start(bf16[27,4,256]{2,1,0:T(4,128)(2,1)} %param.5) | copy-start | bytes 165892
  33.3 9.2 %collective-permute-start.7 = (bf16[64,1,1,64]{3,2,0,1:T(2,128)(2,1)S(1)}, bf16[64,1,1,64]{3,2,0,1:T(2,128)(2,1)S(1)}, u32[]{:S(2)}, u32[]{:S(2)}) collective-permute-start(bf16[64,1,1,64]{3,2,0,1:T(2,128)(2,1)S(1)} %get-tuple-element.15), channel_id=1, source_target_pairs={{65,0},{66,1},{67,2},{68,3},{69,4},{70,5},{71,6},{129,64},{130,65}... | collective-permute-start | bytes 24584 | tf_op jit(solution)/shard_map/ppermute | solution.py:27
  80.0 17.1 %copy-start.5 = (bf16[32,2,512]{2,1,0:T(2,128)(2,1)S(1)}, bf16[32,2,512]{2,1,0:T(2,128)(2,1)}, u32[]{:S(2)}) copy-start(bf16[32,2,512]{2,1,0:T(2,128)(2,1)} %param.4) | copy-start | bytes 196612
  82.1 117.9 %all-to-all-start = ((bf16[8,2,13824]{2,1,0:T(2,128)(2,1)}), bf16[8,2,13824]{2,1,0:T(2,128)(2,1)S(1)}, u32[]{:S(2)}, u32[]{:S(2)}) async-start(bf16[8,2,13824]{2,1,0:T(2,128)(2,1)} %reshape.64), calls=%async_computation | async-start | bytes 884736 | tf_op jit(solution)/shard_map/all_to_all | solution.py:78
  96.8 331.6 %all-reduce.6.cloned.1.call-start = ((), (), s32[]{:S(2)}) async-start(), calls=%async_computation.3 | async-start | bytes 1769472
  300.6 1.1 copy-start.1
  307.3 18.6 %copy-start.2 = (bf16[256,4,10,1,8,9]{0,4,5,2,1,3:T(8,128)(2,1)S(1)}, bf16[256,4,10,1,8,9]{0,4,5,2,1,3:T(8,128)(2,1)}, u32[]{:S(2)}) copy-start(bf16[256,4,10,1,8,9]{0,4,5,2,1,3:T(8,128)(2,1)} %copy-done.1) | copy-start | bytes 4423684
  307.3 18.6 %copy-start.4 = (bf16[32,256,27]{1,0,2:T(8,128)(2,1)S(1)}, bf16[32,256,27]{1,0,2:T(8,128)(2,1)}, u32[]{:S(2)}) copy-start(bf16[32,256,27]{1,0,2:T(8,128)(2,1)} %copy.63) | copy-start | bytes 1327108
  307.3 18.6 %copy-start.7 = (pred[8,9]{0,1:T(8,128)(4,1)S(1)}, pred[8,9]{0,1:T(8,128)(4,1)}, u32[]{:S(2)}) copy-start(pred[8,9]{0,1:T(8,128)(4,1)} %constant.13) | copy-start | bytes 220
  325.8 187.7 %all-reduce.4.cloned.1.call-start = ((), (), s32[]{:S(2)}) async-start(), calls=%async_computation.1 | async-start | bytes 221184 | tf_op jit(solution)/shard_map/psum | solution.py:88
  325.9 4.3 copy-start
  335.5 1.0 copy-start.3
Sparse Core Ops, SparseCore 0:
  45.1 244.2 all-gather.2
  325.9 102.4 all-reduce.5
  431.9 81.5 all-reduce.3
where the time goes:
time: 527 us; the launch traced here: 522 us
  waiting for transfers between devices  358 us (68%)
  local copies, waits for them, and re-layouts  45.7 us (9%)
  starting transfers between devices  41 us (8%)
  blocking collectives  31.7 us (6%)
  matrix products  27 us (5%)
  between operations  15.1 us (3%)
    all_to_all x1, waiting for transfers between devices, per_device(): lax.all_to_all(group_weights, 'grp', split_axis=2, concat_axis=1, tiled=T...  99.3 us
    unnamed x4, waiting for transfers between devices  87.6 us
    all_gather x1, waiting for transfers between devices, per_device(): whole = lax.all_gather(haloed(both), 'grp', axis=0, tiled=False)  81.8 us
    psum x1, waiting for transfers between devices, per_device(): filter_grad = lax.psum(rows_part, 'slab') * scale_factor  81.4 us
    all_gather x1, blocking collectives, per_device(): group_weights = lax.all_gather(weights, 'rb', axis=1, tiled=True)  31.7 us
    conv_general_dilated x3, matrix products, correlate(): lax.conv_general_dilated(image, kernel, (1, 1, 1), ((0, 0), (0, 0), (1, 1...  27 us
    unnamed x29, local copies, waits for them, and re-layouts  16.9 us
    ppermute x4, starting transfers between devices, from_offset(): return lax.ppermute(value, ('rb', 'slab'), pairs)  15.9 us
  transfers between devices with their start and end apart: 12, of which 5 were waited for; matrix products, arithmetic and copies ran while one was open for 6% of the time, Pallas kernels for 0%

commit v1 on v0

--- a/solution.py
+++ b/solution.py
@@ -74,7 +74,15 @@
     whole = lax.all_gather(haloed(both), "grp", axis=0, tiled=False)
     whole_in = whole[:, :chan_local].reshape((CH_IN,) + whole.shape[2:])
     whole_grad = whole[:, chan_local:].reshape((CH_OUT,) + whole.shape[2:])
-    group_weights = lax.all_gather(weights, "rb", axis=1, tiled=True)
+    group_weights = jnp.concatenate(
+        lax.all_to_all(
+            jnp.stack(lax.psum(1, axis_name="rb") * [weights]),
+            axis_name="rb",
+            split_axis=0,
+            concat_axis=0,
+        ),
+        axis=1,
+    )
     column_weights = lax.all_to_all(group_weights, "grp", split_axis=2, concat_axis=1, tiled=True)
     out_kernel = jnp.transpose(group_weights, (1, 2, 0)).reshape(chan_local, CH_IN, 3, 3, 3)
     output_sum = correlate(whole_in[None], out_kernel, "NCDHW")

time: 527 us -> 530 us (level)
  waiting for transfers between devices: 358 us -> 377 us
  blocking collectives: 31.7 us -> 16.8 us
    all_gather x1, waiting for transfers between devices: 81.8 us -> 145 us  [per_device(): whole = lax.all_gather(haloed(both), 'grp', axis=0, tiled=False)]
    all_to_all x1, waiting for transfers between devices: 99.3 us -> 57 us  [per_device(): lax.all_to_all(group_weights, 'grp', split_axis=2, concat_axis=1, tiled=T...]
    all_gather x1 -> x0, blocking collectives: 31.7 us -> none  [per_device(): group_weights = lax.all_gather(weights, 'rb', axis=1, tiled=True)]
    all_to_all x0 -> x1, blocking collectives: none -> 16.8 us  [per_device(): lax.all_to_all(jnp.stack(lax.psum(1, axis_name='rb') * [weights]), axis_n...]
    unnamed x29 -> x26, local copies, waits for them, and re-layouts: 16.9 us -> 16.2 us
  transfers between devices with their start and end apart: 12 -> 12, of which waited for: 5 -> 5; matrix products, arithmetic and copies ran while one was open for 6% -> 5% of each run, Pallas kernels for 0% -> 0%
where the time goes in v1:
time: 530 us; the launch traced here: 525 us
  waiting for transfers between devices  377 us (71%)
  local copies, waits for them, and re-layouts  44.8 us (8%)
  starting transfers between devices  41.2 us (8%)
  matrix products  27.1 us (5%)
  blocking collectives  16.8 us (3%)
  between operations  15.1 us (3%)
    all_gather x1, waiting for transfers between devices, per_device(): whole = lax.all_gather(haloed(both), 'grp', axis=0, tiled=False)  145 us
    unnamed x4, waiting for transfers between devices  86.1 us
    psum x1, waiting for transfers between devices, per_device(): filter_grad = lax.psum(rows_part, 'slab') * scale_factor  81.4 us
    all_to_all x1, waiting for transfers between devices, per_device(): lax.all_to_all(group_weights, 'grp', split_axis=2, concat_axis=1, tiled=T...  57 us
    conv_general_dilated x3, matrix products, correlate(): lax.conv_general_dilated(image, kernel, (1, 1, 1), ((0, 0), (0, 0), (1, 1...  27.1 us
    all_to_all x1, blocking collectives, per_device(): lax.all_to_all(jnp.stack(lax.psum(1, axis_name='rb') * [weights]), axis_n...  16.8 us
    unnamed x26, local copies, waits for them, and re-layouts  16.2 us
    ppermute x4, starting transfers between devices, from_offset(): return lax.ppermute(value, ('rb', 'slab'), pairs)  15.9 us
  transfers between devices with their start and end apart: 12, of which 5 were waited for; matrix products, arithmetic and copies ran while one was open for 5% of the time, Pallas kernels for 0%

profile of v1, /device:TPU:1, one launch (start us, length us, event | category | flops | bytes accessed | tf_op | source)
XLA Modules:
  0.0 525.2 jit_solution(15586441641353088973)
XLA Ops:
  8.6 7.4 %collective-permute-start = (bf16[64,1,1,64]{3,2,0,1:T(2,128)(2,1)S(1)}, bf16[64,1,1,64]{3,2,0,1:T(2,128)(2,1)S(1)}, u32[]{:S(2)}, u32[]{:S(2)}) collective-permute-start(bf16[64,1,1,64]{3,2,0,1:T(2,128)(2,1)S(1)} %get-tuple-element.14), channel_id=1, source_target_pairs={{0,65},{1,66},{2,67},{3,68},{4,69},{5,70},{6,71},{64,129},{65,130}... | collective-permute-start | bytes 24584 | tf_op jit(solution)/shard_map/ppermute | solution.py:27
  16.0 1.3 collective-permute-start.2
  17.3 5.8 %collective-permute-start.5 = (bf16[64,1,1,64]{3,2,0,1:T(2,128)(2,1)S(1)}, bf16[64,1,1,64]{3,2,0,1:T(2,128)(2,1)S(1)}, u32[]{:S(2)}, u32[]{:S(2)}) collective-permute-start(bf16[64,1,1,64]{3,2,0,1:T(2,128)(2,1)S(1)} %get-tuple-element.16), channel_id=1, source_target_pairs={{1,64},{2,65},{3,66},{4,67},{5,68},{6,69},{7,70},{65,128},{66,129}... | collective-permute-start | bytes 24584 | tf_op jit(solution)/shard_map/ppermute | solution.py:27
  23.1 2.8 collective-permute-start.1
  25.9 1.9 collective-permute-start.6
  27.9 4.1 collective-permute-start.3
  32.0 1.3 collective-permute-start.4
  33.3 1.4 collective-permute-start.7
  34.7 7.8 %collective-permute-done.7 = bf16[64,1,1,64]{3,2,0,1:T(2,128)(2,1)S(1)} collective-permute-done((bf16[64,1,1,64]{3,2,0,1:T(2,128)(2,1)S(1)}, bf16[64,1,1,64]{3,2,0,1:T(2,128)(2,1)S(1)}, u32[]{:S(2)}, u32[]{:S(2)}) %collective-permute-start.7) | collective-permute-done | bytes 8224 | tf_op jit(solution)/shard_map/ppermute | solution.py:27
  43.2 1.7 copy.55
  45.1 16.8 %all_to_all.23 = bf16[8,27,4,256]{3,2,1,0:T(4,128)(2,1)S(1)} all-to-all(bf16[8,27,4,256]{3,2,1,0:T(4,128)(2,1)S(1)} %stack.2), channel_id=1, replica_groups=mesh['rb'=8,'grp'=8,'slab'=8] {'rb'}, dimensions={0} | all-to-all | bytes 884736 | tf_op jit(solution)/shard_map/all_to_all | solution.py:78
  62.3 3.0 copy.67
  65.3 2.1 reshape.74
  67.4 14.8 %all-to-all-start.1 = ((bf16[8,2,13824]{2,1,0:T(2,128)(2,1)}), bf16[8,2,13824]{2,1,0:T(2,128)(2,1)S(1)}, u32[]{:S(2)}, u32[]{:S(2)}) async-start(bf16[8,2,13824]{2,1,0:T(2,128)(2,1)} %reshape.74), calls=%async_computation.1 | async-start | bytes 884736 | tf_op jit(solution)/shard_map/all_to_all | solution.py:86
  85.8 57.0 %all-to-all-done.1 = bf16[8,2,13824]{2,1,0:T(2,128)(2,1)S(1)} async-done(((bf16[8,2,13824]{2,1,0:T(2,128)(2,1)}), bf16[8,2,13824]{2,1,0:T(2,128)(2,1)S(1)}, u32[]{:S(2)}, u32[]{:S(2)}) %all-to-all-start.1) | async-done | bytes 442400 | tf_op jit(solution)/shard_map/all_to_all | solution.py:86
  142.7 1.6 reshape.75
  144.3 2.4 copy.86
  146.8 2.8 all_to_all.20
  149.6 144.7 %all-gather.3.cloned.1.call-done = bf16[512,4,10,64]{3,1,2,0:T(4,128)(2,1)} async-done(((bf16[64,4,10,64]{3,1,2,0:T(4,128)(2,1)}), bf16[512,4,10,64]{3,1,2,0:T(4,128)(2,1)}) %all-gather.3.cloned.1.call-update) | async-done | bytes 2621456 | tf_op jit(solution)/shard_map/all_gather | solution.py:74
  294.3 5.9 %fusion.36 = (bf16[8,32,4,10,64]{4,2,3,1,0:T(4,128)(2,1)}, bf16[8,32,4,10,64]{4,2,3,1,0:T(4,128)(2,1)S(1)}) fusion(bf16[8,64,4,10,64]{4,2,3,1,0:T(4,128)(2,1)} %bitcast.67), kind=kLoop, calls=%fused_computation.34 | loop fusion | bytes 5242880 | tf_op jit(solution)/shard_map/slice | solution.py:76
  300.8 2.5 copy.83
  303.3 1.9 pad.clone
  307.4 5.4 %copy.71 = bf16[256,1,4,10,64]{0,1,4,3,2:T(2,128)(2,1)} copy(bf16[256,1,4,10,64]{4,0,3,2,1:T(8,128)(2,1)S(1)} %bitcast.60) | data formatting | bytes 2621440 | tf_op jit(solution)/shard_map/broadcast_in_dim;reshape | solution.py:90
  312.9 18.6 %fusion.40 = f32[256,32,3,3,3]{0,1,4,3,2:T(8,128)} fusion(bf16[256,1,4,10,64]{0,1,4,3,2:T(2,128)(2,1)} %copy.71, bf16[32,1,2,8,64]{0,1,4,3,2:T(2,128)(2,1)} %copy.72), kind=kOutput, calls=%fused_computation.38 | convolution fusion | flops 448266240 | bytes 2260992 | tf_op jit(solution)/shard_map/conv_general_dilated | solution.py:55
  331.6 4.3 fusion.22
  336.6 2.7 copy.84
  339.3 1.9 pad.2.clone
  341.5 4.3 fusion.25
  345.8 86.0 %all-reduce.6.cloned.1.call-done = f32[27,32,256]{2,1,0:T(8,128)} async-done(((f32[27,32,256]{2,1,0:T(8,128)}), f32[27,32,256]{2,1,0:T(8,128)}) %all-reduce.6.cloned.1.call-update) | async-done | bytes 884752
  431.9 1.6 constant_dynamic-slice_fusion
  435.5 81.4 %all-reduce.4.cloned.1.call-done = f32[27,4,256]{2,1,0:T(4,128)} async-done(((f32[27,4,256]{2,1,0:T(4,128)}), f32[27,4,256]{2,1,0:T(4,128)}) %all-reduce.4.cloned.1.call-update) | async-done | bytes 110608 | tf_op jit(solution)/shard_map/psum | solution.py:96
  516.9 1.6 broadcast_multiply_fusion
  (55 shorter events, 11.4 us)
Async XLA Ops:
  7.2 287.1 %all-gather.3.cloned.1.call-start = ((), (), s32[]{:S(2)}) async-start(), calls=%async_computation.3 | async-start | bytes 5898240 | tf_op jit(solution)/shard_map/all_gather | solution.py:74
  8.6 19.3 %collective-permute-start = (bf16[64,1,1,64]{3,2,0,1:T(2,128)(2,1)S(1)}, bf16[64,1,1,64]{3,2,0,1:T(2,128)(2,1)S(1)}, u32[]{:S(2)}, u32[]{:S(2)}) collective-permute-start(bf16[64,1,1,64]{3,2,0,1:T(2,128)(2,1)S(1)} %get-tuple-element.14), channel_id=1, source_target_pairs={{0,65},{1,66},{2,67},{3,68},{4,69},{5,70},{6,71},{64,129},{65,130}... | collective-permute-start | bytes 24584 | tf_op jit(solution)/shard_map/ppermute | solution.py:27
  16.0 16.0 %collective-permute-start.2 = (bf16[64,1,1,64]{3,2,0,1:T(2,128)(2,1)S(1)}, bf16[64,1,1,64]{3,2,0,1:T(2,128)(2,1)S(1)}, u32[]{:S(2)}, u32[]{:S(2)}) collective-permute-start(bf16[64,1,1,64]{3,2,0,1:T(2,128)(2,1)S(1)} %get-tuple-element.17), channel_id=1, source_target_pairs={{64,1},{65,2},{66,3},{67,4},{68,5},{69,6},{70,7},{128,65},{129,66}... | collective-permute-start | bytes 24584 | tf_op jit(solution)/shard_map/ppermute | solution.py:27
  17.3 16.0 %collective-permute-start.5 = (bf16[64,1,1,64]{3,2,0,1:T(2,128)(2,1)S(1)}, bf16[64,1,1,64]{3,2,0,1:T(2,128)(2,1)S(1)}, u32[]{:S(2)}, u32[]{:S(2)}) collective-permute-start(bf16[64,1,1,64]{3,2,0,1:T(2,128)(2,1)S(1)} %get-tuple-element.16), channel_id=1, source_target_pairs={{1,64},{2,65},{3,66},{4,67},{5,68},{6,69},{7,70},{65,128},{66,129}... | collective-permute-start | bytes 24584 | tf_op jit(solution)/shard_map/ppermute | solution.py:27
  23.1 19.5 %collective-permute-start.1 = (bf16[64,1,8,64]{3,2,0,1:T(8,128)(2,1)S(1)}, bf16[64,1,8,64]{3,2,0,1:T(8,128)(2,1)S(1)}, u32[]{:S(2)}, u32[]{:S(2)}) collective-permute-start(bf16[64,1,8,64]{3,2,0,1:T(8,128)(2,1)S(1)} %get-tuple-element.18), channel_id=1, source_target_pairs={{0,1},{1,2},{2,3},{3,4},{4,5},{5,6},{6,7},{8,9},{9,10},{10,11},{11... | collective-permute-start | bytes 196616 | tf_op jit(solution)/shard_map/ppermute | solution.py:21
  25.9 16.7 %collective-permute-start.6 = (bf16[64,1,8,64]{3,2,0,1:T(8,128)(2,1)S(1)}, bf16[64,1,8,64]{3,2,0,1:T(8,128)(2,1)S(1)}, u32[]{:S(2)}, u32[]{:S(2)}) collective-permute-start(bf16[64,1,8,64]{3,2,0,1:T(8,128)(2,1)S(1)} %get-tuple-element.19), channel_id=1, source_target_pairs={{1,0},{2,1},{3,2},{4,3},{5,4},{6,5},{7,6},{9,8},{10,9},{11,10},{12... | collective-permute-start | bytes 196616 | tf_op jit(solution)/shard_map/ppermute | solution.py:21
  27.9 14.6 %collective-permute-start.3 = (bf16[64,2,1,64]{3,2,0,1:T(2,128)(2,1)S(1)}, bf16[64,2,1,64]{3,2,0,1:T(2,128)(2,1)S(1)}, u32[]{:S(2)}, u32[]{:S(2)}) collective-permute-start(bf16[64,2,1,64]{3,2,0,1:T(2,128)(2,1)S(1)} %get-tuple-element.20), channel_id=1, source_target_pairs={{0,64},{64,128},{128,192},{192,256},{256,320},{320,384},{384,448},... | collective-permute-start | bytes 49160 | tf_op jit(solution)/shard_map/ppermute | solution.py:18
  32.0 10.6 %collective-permute-start.4 = (bf16[64,2,1,64]{3,2,0,1:T(2,128)(2,1)S(1)}, bf16[64,2,1,64]{3,2,0,1:T(2,128)(2,1)S(1)}, u32[]{:S(2)}, u32[]{:S(2)}) collective-permute-start(bf16[64,2,1,64]{3,2,0,1:T(2,128)(2,1)S(1)} %get-tuple-element.21), channel_id=1, source_target_pairs={{64,0},{128,64},{192,128},{256,192},{320,256},{384,320},{448,384},... | collective-permute-start | bytes 49160 | tf_op jit(solution)/shard_map/ppermute | solution.py:18
  33.3 11.7 %copy-start.5 = (bf16[27,4,256]{2,1,0:T(4,128)(2,1)S(1)}, bf16[27,4,256]{2,1,0:T(4,128)(2,1)}, u32[]{:S(2)}) copy-start(bf16[27,4,256]{2,1,0:T(4,128)(2,1)} %param.5) | copy-start | bytes 165892
  33.3 9.2 %collective-permute-start.7 = (bf16[64,1,1,64]{3,2,0,1:T(2,128)(2,1)S(1)}, bf16[64,1,1,64]{3,2,0,1:T(2,128)(2,1)S(1)}, u32[]{:S(2)}, u32[]{:S(2)}) collective-permute-start(bf16[64,1,1,64]{3,2,0,1:T(2,128)(2,1)S(1)} %get-tuple-element.15), channel_id=1, source_target_pairs={{65,0},{66,1},{67,2},{68,3},{69,4},{70,5},{71,6},{129,64},{130,65}... | collective-permute-start | bytes 24584 | tf_op jit(solution)/shard_map/ppermute | solution.py:27
  65.3 17.3 %copy-start.4 = (bf16[32,2,512]{2,1,0:T(2,128)(2,1)S(1)}, bf16[32,2,512]{2,1,0:T(2,128)(2,1)}, u32[]{:S(2)}) copy-start(bf16[32,2,512]{2,1,0:T(2,128)(2,1)} %param.4) | copy-start | bytes 196612
  67.4 75.4 %all-to-all-start.1 = ((bf16[8,2,13824]{2,1,0:T(2,128)(2,1)}), bf16[8,2,13824]{2,1,0:T(2,128)(2,1)S(1)}, u32[]{:S(2)}, u32[]{:S(2)}) async-start(bf16[8,2,13824]{2,1,0:T(2,128)(2,1)} %reshape.74), calls=%async_computation.1 | async-start | bytes 884736 | tf_op jit(solution)/shard_map/all_to_all | solution.py:86
  82.2 349.6 %all-reduce.6.cloned.1.call-start = ((), (), s32[]{:S(2)}) async-start(), calls=%async_computation.4 | async-start | bytes 1769472
  305.5 1.1 copy-start.1
  312.9 18.7 %copy-start.2 = (bf16[256,4,10,1,8,9]{0,4,5,2,1,3:T(8,128)(2,1)S(1)}, bf16[256,4,10,1,8,9]{0,4,5,2,1,3:T(8,128)(2,1)}, u32[]{:S(2)}) copy-start(bf16[256,4,10,1,8,9]{0,4,5,2,1,3:T(8,128)(2,1)} %copy-done.1) | copy-start | bytes 4423684
  312.9 18.7 %copy-start.3 = (bf16[256,4,10,1,7,2]{0,4,5,2,1,3:T(8,128)(2,1)S(1)}, bf16[256,4,10,1,7,2]{0,4,5,2,1,3:T(8,128)(2,1)}, u32[]{:S(2)}) copy-start(bf16[256,4,10,1,7,2]{0,4,5,2,1,3:T(8,128)(2,1)} %slice.61) | copy-start | bytes 860164
  312.9 18.7 %copy-start.6 = (pred[8,9]{0,1:T(8,128)(4,1)S(1)}, pred[8,9]{0,1:T(8,128)(4,1)}, u32[]{:S(2)}) copy-start(pred[8,9]{0,1:T(8,128)(4,1)} %constant.13) | copy-start | bytes 220
  331.5 185.4 %all-reduce.4.cloned.1.call-start = ((), (), s32[]{:S(2)}) async-start(), calls=%async_computation.2 | async-start | bytes 221184 | tf_op jit(solution)/shard_map/psum | solution.py:96
  331.6 4.3 copy-start
Sparse Core Ops, SparseCore 0:
  45.1 249.1 all-gather.2
  331.6 100.1 all-reduce.5
  435.4 81.5 all-reduce.3
